TPU v7x, 512 devices: a whole 4x4x16 slice. The times are simulated.
512 devices in a mesh: dp: 16 (over y_lo, x, core), mp: 32 (over z, y_hi).
Axes of the slice: x: 4, y: 4 (y_hi: 2, y_lo: 2; y = y_hi * 2 + y_lo), z: 16, core: 2. Of those that a mesh axis runs over, the one named last changes fastest.
Arguments:
- hidden_states: bfloat16 [8192, 2560], P(('dp', 'mp')), may hold values from -60 to 60
- norm_gain: float32 [2560], replicated, may hold values from 0.5 to 1.5
- head_weight: bfloat16 [2560, 65536], P(None, ('dp', 'mp')), may hold values from -64 to 64
- target_ids: int32 [8192], P(('dp', 'mp')), may hold values from 0 to 65535
- response_mask: int32 [8192], P(('dp', 'mp')), may hold values from 0 to 1, as said below
Outputs:
- token_logprob: float32 [8192], P(('dp', 'mp'))
- token_entropy: float32 [8192], P(('dp', 'mp'))
Inputs may be any that keep to these rules, and one draw needn't show every extreme that they name: `response_mask`: each aligned run of 256 positions is one rollout: a prompt of 0s, then one span of 1s, then padding 0s.
All inputs are finite; a program needn't handle non-finite values.
Results may differ from a plain program's by a relative error of at most 0.0048.
Values may be sent and summed in bfloat16 or wider, within the bound.
No kernel may reach another device: no remote copies, remote signals or barrier semaphores. Data moves between devices by JAX's collectives and lax.ppermute only.
A program may use at most 64 MiB of HBM per device.

v0:
```python
import jax
import jax.numpy as jnp
from jax import lax
from jax.sharding import PartitionSpec as P

lowest_start = -1e30


def combined_all(value, axis, join):
    pieces = jax.tree.map(lambda part: lax.all_gather(part, axis), value)
    head = jax.tree.map(lambda part: part[0], pieces)
    tail = jax.tree.map(lambda part: part[1:], pieces)
    total, _ = lax.scan(lambda total, share: (join(total, share), None), head, tail)
    return total


def combine_stats(earlier, later):
    top_first, sum_first, moment_first, chosen_first = earlier
    top_second, sum_second, moment_second, chosen_second = later
    top_new = jnp.maximum(top_first, top_second)
    factor_first = jnp.exp(top_first - top_new)
    factor_second = jnp.exp(top_second - top_new)
    return (
        top_new,
        sum_first * factor_first + sum_second * factor_second,
        moment_first * factor_first + moment_second * factor_second,
        chosen_first + chosen_second,
    )


def start_stats(row_count):
    zeros = jnp.zeros((row_count,), jnp.float32)
    return (jnp.full((row_count,), lowest_start, jnp.float32), zeros, zeros, zeros)


def add_columns(running, token_rows, token_targets, column_piece, column_ids):
    logits = jnp.dot(token_rows, column_piece, preferred_element_type=jnp.float32)
    piece_top = jnp.max(logits, axis=1)
    shifted = jnp.exp(logits - piece_top[:, None])
    target_hit = token_targets[:, None] == column_ids[None, :]
    piece_stats = (
        piece_top,
        jnp.sum(shifted, axis=1),
        jnp.sum(shifted * logits, axis=1),
        jnp.sum(jnp.where(target_hit, logits, 0.0), axis=1),
    )
    return combine_stats(running, piece_stats)


def local(hidden_states, norm_gain, head_weight, target_ids, response_mask):
    states = hidden_states.astype(jnp.float32)
    mean_square = jnp.mean(states * states, axis=1, keepdims=True)
    normed = (states * lax.rsqrt(mean_square + 1e-06) * norm_gain[None, :]).astype(jnp.bfloat16)
    mp_count = lax.axis_size("mp")
    mp_index = lax.axis_index("mp")
    shard_cols = head_weight.shape[1]
    send_count = normed.shape[0]
    group_states, group_targets = (
        lax.all_gather(normed, "mp", axis=0, tiled=True),
        lax.all_gather(target_ids, "mp", axis=0, tiled=True),
    )
    column_piece = lax.all_gather(head_weight, "dp", axis=1, tiled=True)
    positions = jnp.arange(column_piece.shape[1], dtype=jnp.int32)
    owners = positions // shard_cols
    column_ids = (owners * mp_count + mp_index) * shard_cols + positions % shard_cols
    partial_stats = add_columns(
        start_stats(group_states.shape[0]), group_states, group_targets, column_piece, column_ids
    )
    merged = combined_all(partial_stats, "mp", combine_stats)
    first_row = mp_index * send_count
    top_logit, weight_total, moment, chosen = [
        lax.dynamic_slice_in_dim(member, first_row, send_count) for member in merged
    ]
    log_total = top_logit + jnp.log(weight_total)
    logprob = chosen - log_total
    entropy = log_total - moment / weight_total
    scored = response_mask.astype(jnp.float32)
    return (logprob * scored, entropy * scored)


def solution(mesh):
    return jax.shard_map(
        local,
        mesh=mesh,
        in_specs=(
            P(("dp", "mp"), None),
            P(),
            P(None, ("dp", "mp")),
            P(("dp", "mp")),
            P(("dp", "mp")),
        ),
        out_specs=(P(("dp", "mp")), P(("dp", "mp"))),
        check_vma=False,
    )
```

profile of v0, /device:TPU:16, one launch (start us, length us, event | category | flops | bytes accessed | tf_op | source)
XLA Modules:
  0.0 556.4 jit_solution(13439225483847453185)
XLA Ops:
  7.2 0.0 all-gather.8.cloned.1.call-start
  7.2 1.0 fusion.1
  8.2 1.6 fusion.3
  9.9 0.0 all-gather.8.cloned.1.call-update
  9.9 0.0 all-gather.10.cloned.1.call-start
  9.9 0.7 all-gather.10.cloned.1.call-update
  10.6 1.3 dynamic-slice
  12.6 0.9 dynamic-update-slice
  13.4 30.9 %all-reduce = s32[512]{0:T(512)S(1)} all-reduce(s32[512]{0:T(512)S(1)} %dynamic-update-slice), channel_id=1, replica_groups=mesh['dp'=16,'mp'=32] {'mp'}, use_global_device_ids=true, to_apply=%add | all-reduce | flops 512 | bytes 4096
  44.3 121.9 %all-gather.8.cloned.1.call-done = bf16[512,2560]{1,0:T(8,128)(2,1)} async-done(((bf16[16,2560]{1,0:T(8,128)(2,1)}), bf16[512,2560]{1,0:T(8,128)(2,1)}) %all-gather.8.cloned.1.call-update) | async-done | bytes 2621456 | tf_op jit(solution)/shard_map/all_gather | solution.py:59
  166.3 74.4 %all-gather.10.cloned.1.call-done = bf16[2560,2048]{1,0:T(8,128)(2,1)} async-done(((bf16[2560,128]{1,0:T(8,128)(2,1)}), bf16[2560,2048]{1,0:T(8,128)(2,1)}) %all-gather.10.cloned.1.call-update) | async-done | bytes 10485776 | tf_op jit(solution)/shard_map/all_gather | solution.py:62
  240.7 9.2 %fusion.15 = (f32[512]{0:T(512)S(1)}, f32[512,2048]{1,0:T(8,128)S(1)}) fusion(bf16[512,2560]{1,0:T(8,128)(2,1)} %all-gather.8.cloned.1.call-done, bf16[2560,2048]{1,0:T(8,128)(2,1)} %all-gather.10.cloned.1.call-done), kind=kOutput, calls=%fused_computation.45 | convolution fusion | flops 5369757184 | bytes 17303552 | tf_op jit(solution)/shard_map/dot_general | solution.py:37
  249.9 0.0 copy-start
  249.9 1.9 multiply_reduce_fusion
  251.8 73.0 %all-gather.3 = f32[32,1,512]{2,1,0:T(1,128)S(1)} all-gather(f32[1,1,512]{2,1,0:T(1,128)S(1)} %get-tuple-element.85), channel_id=1, replica_groups=mesh['dp'=16,'mp'=32] {'mp'}, dimensions={0}, use_global_device_ids=true | all-gather | bytes 67584 | tf_op jit(solution)/shard_map/all_gather | solution.py:10
  324.8 75.5 %all-gather.1 = f32[32,1,512]{2,1,0:T(1,128)S(1)} all-gather(f32[1,1,512]{2,1,0:T(1,128)S(1)} %get-tuple-element.87), channel_id=1, replica_groups=mesh['dp'=16,'mp'=32] {'mp'}, dimensions={0}, use_global_device_ids=true | all-gather | bytes 67584 | tf_op jit(solution)/shard_map/all_gather | solution.py:10
  400.3 70.7 %all-gather.2 = f32[32,1,512]{2,1,0:T(1,128)S(1)} all-gather(f32[1,1,512]{2,1,0:T(1,128)S(1)} %get-tuple-element.86), channel_id=1, replica_groups=mesh['dp'=16,'mp'=32] {'mp'}, dimensions={0}, use_global_device_ids=true | all-gather | bytes 67584 | tf_op jit(solution)/shard_map/all_gather | solution.py:10
  471.0 74.2 %all-gather.4 = f32[32,1,512]{2,1,0:T(1,128)S(1)} all-gather(f32[1,1,512]{2,1,0:T(1,128)S(1)} %bitcast.54), channel_id=2, replica_groups=mesh['dp'=16,'mp'=32] {'mp'}, dimensions={0}, use_global_device_ids=true | all-gather | bytes 67584 | tf_op jit(solution)/shard_map/all_gather | solution.py:10
  545.3 3.6 while.16
  549.0 0.0 copy-done
  549.0 0.6 subtract_multiply_fusion
  (202 shorter events, 2.3 us)
Async XLA Ops:
  7.2 159.1 %all-gather.8.cloned.1.call-start = ((), (), s32[]{:S(2)}) async-start(), calls=%async_computation | async-start | bytes 2703360 | tf_op jit(solution)/shard_map/all_gather | solution.py:59
  9.9 230.8 %all-gather.10.cloned.1.call-start = ((), (), s32[]{:S(2)}) async-start(), calls=%async_computation.1 | async-start | bytes 11141120 | tf_op jit(solution)/shard_map/all_gather | solution.py:62
  249.9 299.1 %copy-start = (s32[16]{0:T(128)S(1)}, s32[16]{0:T(128)}, u32[]{:S(2)}) copy-start(s32[16]{0:T(128)} %param.11) | copy-start | bytes 196
Sparse Core Ops, SparseCore 0:
  11.1 155.1 all-gather.7
  168.3 72.2 all-gather.9
where the time goes:
time: 557 us; the launch traced here: 556 us
  blocking collectives  324 us (58%)
  waiting for transfers between devices  197 us (35%)
  between operations  14.8 us (3%)
  matrix products  9.23 us (2%)
  other arithmetic  6.51 us (1%)
    all_gather x4, blocking collectives, combined_all(): pieces = jax.tree.map(lambda part: lax.all_gather(part, axis), value)  293 us
    all_gather x1, waiting for transfers between devices, local(): lax.all_gather(normed, 'mp', axis=0, tiled=True)  122 us
    all_gather x1, waiting for transfers between devices, local(): column_piece = lax.all_gather(head_weight, 'dp', axis=1, tiled=True)  74.4 us
    unnamed x1, blocking collectives  30.9 us
  transfers between devices with their start and end apart: 2, of which 2 were waited for; matrix products, arithmetic and copies ran while one was open for 0% of the time, Pallas kernels for 0%

commit v1 on v0

--- a/solution.py
+++ b/solution.py
@@ -59,7 +59,9 @@
         lax.all_gather(normed, "mp", axis=0, tiled=True),
         lax.all_gather(target_ids, "mp", axis=0, tiled=True),
     )
-    column_piece = lax.all_gather(head_weight, "dp", axis=1, tiled=True)
+    column_piece = jnp.concatenate(
+        lax.all_to_all(jnp.stack([head_weight] * lax.axis_size("dp")), "dp", 0, 0), axis=1
+    )
     positions = jnp.arange(column_piece.shape[1], dtype=jnp.int32)
     owners = positions // shard_cols
     column_ids = (owners * mp_count + mp_index) * shard_cols + positions % shard_cols

time: 557 us -> 529 us (0.950)
  the two profiles are of different devices: /device:TPU:16 before, /device:TPU:4 now
where the time goes in v1:
time: 529 us
  blocking collectives  385 us (73%)
  waiting for transfers between devices  94.4 us (18%)
  between operations  14.8 us (3%)
  starting transfers between devices  10.6 us (2%)
  matrix products  9.29 us (2%)
  local copies, waits for them, and re-layouts  8.64 us (2%)
    all_gather x4, blocking collectives, combined_all(): pieces = jax.tree.map(lambda part: lax.all_gather(part, axis), value)  290 us
    unnamed x1, blocking collectives  95.1 us
    all_gather x1, waiting for transfers between devices, local(): lax.all_gather(normed, 'mp', axis=0, tiled=True)  94.4 us
  transfers between devices with their start and end apart: 2, of which 1 were waited for; matrix products, arithmetic and copies ran while one was open for 0% of the time, Pallas kernels for 0%

profile of v1, /device:TPU:4, one launch (start us, length us, event | category | flops | bytes accessed | tf_op | source)
XLA Modules:
  0.0 528.8 jit_solution(6415592467981843410)
XLA Ops:
  7.2 1.3 copy.8
  8.5 4.8 stack.2
  13.3 0.0 copy-start
  13.3 0.0 copy-start.1
  13.3 0.0 copy-start.3
  13.4 10.6 %all-to-all-start = ((bf16[16,2560,128]{1,2,0:T(8,128)(2,1)}), bf16[16,2560,128]{1,2,0:T(8,128)(2,1)}, u32[]{:S(2)}, u32[]{:S(2)}) async-start(bf16[16,2560,128]{1,2,0:T(8,128)(2,1)} %stack.2), calls=%async_computation | async-start | bytes 20971520 | tf_op jit(solution)/shard_map/all_to_all | solution.py:63
  23.9 0.0 all-gather.7.cloned.1.call-start
  24.0 0.0 copy-done
  24.0 0.1 fusion.1
  24.1 0.0 copy-done.1
  24.1 0.7 fusion.3
  24.8 0.0 all-gather.7.cloned.1.call-update
  24.9 1.3 dynamic-slice
  26.8 0.0 copy-done.3
  26.8 0.2 dynamic-update-slice
  27.1 95.1 %all-reduce = s32[512]{0:T(512)S(1)} all-reduce(s32[512]{0:T(512)S(1)} %dynamic-update-slice), channel_id=1, replica_groups=mesh['dp'=16,'mp'=32] {'mp'}, use_global_device_ids=true, to_apply=%add | all-reduce | flops 512 | bytes 4096
  122.2 94.4 %all-gather.7.cloned.1.call-done = bf16[512,2560]{1,0:T(8,128)(2,1)} async-done(((bf16[16,2560]{1,0:T(8,128)(2,1)}), bf16[512,2560]{1,0:T(8,128)(2,1)}) %all-gather.7.cloned.1.call-update) | async-done | bytes 2621456 | tf_op jit(solution)/shard_map/all_gather | solution.py:59
  216.6 0.0 all-to-all-done
  216.6 9.3 %fusion.15 = (f32[512]{0:T(512)S(1)}, f32[512,2048]{1,0:T(8,128)S(1)}) fusion(bf16[512,2560]{1,0:T(8,128)(2,1)} %all-gather.7.cloned.1.call-done, bf16[2560,2048]{0,1:T(8,128)(2,1)} %bitcast.5), kind=kOutput, calls=%fused_computation.45 | convolution fusion | flops 5369757184 | bytes 17303552 | tf_op jit(solution)/shard_map/dot_general | solution.py:37
  225.9 0.0 copy-start.2
  225.9 1.7 multiply_reduce_fusion
  227.7 72.9 %all-gather.2 = f32[32,1,512]{2,1,0:T(1,128)S(1)} all-gather(f32[1,1,512]{2,1,0:T(1,128)S(1)} %get-tuple-element.86), channel_id=1, replica_groups=mesh['dp'=16,'mp'=32] {'mp'}, dimensions={0}, use_global_device_ids=true | all-gather | bytes 67584 | tf_op jit(solution)/shard_map/all_gather | solution.py:10
  300.6 72.1 %all-gather.3 = f32[32,1,512]{2,1,0:T(1,128)S(1)} all-gather(f32[1,1,512]{2,1,0:T(1,128)S(1)} %get-tuple-element.85), channel_id=1, replica_groups=mesh['dp'=16,'mp'=32] {'mp'}, dimensions={0}, use_global_device_ids=true | all-gather | bytes 67584 | tf_op jit(solution)/shard_map/all_gather | solution.py:10
  372.7 72.9 %all-gather.1 = f32[32,1,512]{2,1,0:T(1,128)S(1)} all-gather(f32[1,1,512]{2,1,0:T(1,128)S(1)} %get-tuple-element.87), channel_id=1, replica_groups=mesh['dp'=16,'mp'=32] {'mp'}, dimensions={0}, use_global_device_ids=true | all-gather | bytes 67584 | tf_op jit(solution)/shard_map/all_gather | solution.py:10
  445.6 72.1 %all-gather.4 = f32[32,1,512]{2,1,0:T(1,128)S(1)} all-gather(f32[1,1,512]{2,1,0:T(1,128)S(1)} %bitcast.57), channel_id=2, replica_groups=mesh['dp'=16,'mp'=32] {'mp'}, dimensions={0}, use_global_device_ids=true | all-gather | bytes 67584 | tf_op jit(solution)/shard_map/all_gather | solution.py:10
  517.7 3.6 while.16
  521.4 0.0 copy-done.2
  521.4 0.6 subtract_multiply_fusion
  (202 shorter events, 2.3 us)
Async XLA Ops:
  13.3 10.6 %copy-start = (bf16[16,2560]{1,0:T(8,128)(2,1)S(1)}, bf16[16,2560]{1,0:T(8,128)(2,1)}, u32[]{:S(2)}) copy-start(bf16[16,2560]{1,0:T(8,128)(2,1)} %param.7) | copy-start | bytes 245764
  13.3 10.8 %copy-start.1 = (f32[2560]{0:T(1024)S(1)}, f32[2560]{0:T(1024)}, u32[]{:S(2)}) copy-start(f32[2560]{0:T(1024)} %param.8) | copy-start | bytes 30724
  13.3 13.5 %copy-start.3 = (s32[16]{0:T(128)S(1)}, s32[16]{0:T(128)}, u32[]{:S(2)}) copy-start(s32[16]{0:T(128)} %param.10) | copy-start | bytes 196
  13.4 203.3 %all-to-all-start = ((bf16[16,2560,128]{1,2,0:T(8,128)(2,1)}), bf16[16,2560,128]{1,2,0:T(8,128)(2,1)}, u32[]{:S(2)}, u32[]{:S(2)}) async-start(bf16[16,2560,128]{1,2,0:T(8,128)(2,1)} %stack.2), calls=%async_computation | async-start | bytes 20971520 | tf_op jit(solution)/shard_map/all_to_all | solution.py:63
  23.9 192.7 %all-gather.7.cloned.1.call-start = ((), (), s32[]{:S(2)}) async-start(), calls=%async_computation.1 | async-start | bytes 2703360 | tf_op jit(solution)/shard_map/all_gather | solution.py:59
  225.9 295.4 %copy-start.2 = (s32[16]{0:T(128)S(1)}, s32[16]{0:T(128)}, u32[]{:S(2)}) copy-start(s32[16]{0:T(128)} %param.11) | copy-start | bytes 196
Sparse Core Ops, SparseCore 0:
  27.8 188.7 all-gather.6
